TPU v7x, 256 devices: a whole 4x4x8 slice. The times are simulated.
256 devices in a mesh: px: 32 (over z, x_hi, core), py: 8 (over y, x_lo).
Axes of the slice: x: 4 (x_hi: 2, x_lo: 2; x = x_hi * 2 + x_lo), y: 4, z: 8, core: 2. Of those that a mesh axis runs over, the one named last changes fastest.
Arguments:
- table: float32 [25, 50, 1000], replicated, may hold values from -1 to 1
- charge: float32 [128, 32, 8], P('px', 'py'), may hold values from 0.1 to 1
- hit_bins: int32 [128, 32, 8], P('px', 'py'), may hold values from 0 to 49
- hit_ticks: int32 [128, 32, 8], P('px', 'py'), may hold values from 0 to 23
- active: int32 [128, 32], P('px', 'py'), may hold values 0 or 1
- measured: bfloat16 [128, 32, 1024], P('px', 'py'), may hold values from -6 to 6
- row_module: int32 [128], replicated, may hold values from 0 to 6, as said below
- col_module: int32 [32], replicated, may hold values from 0 to 4, as said below
Outputs:
- current: bfloat16 [128, 32, 1024], P('px', 'py')
- table_grad: float32 [25, 50, 1000], P(None, None, 'py')
Inputs may be any that keep to these rules, and one draw needn't show every extreme that they name: `row_module`: starts at 0 and never falls; it rises by one at 6 rows. `col_module`: starts at 0 and never falls; it rises by one at 4 columns.
All inputs are finite; a program needn't handle non-finite values. No bound on the sum of `active` on one device may be relied on, other than what follows from the above.
Results may differ from a plain program's by a relative error of at most 0.014.
Values may be sent and summed in bfloat16 or wider, within the bound.
No kernel may reach another device: no remote copies, remote signals or barrier semaphores. Data moves between devices by JAX's collectives and lax.ppermute only.
A program may use at most 128 MiB of HBM per device.

v0:
```python
import jax
import jax.numpy as jnp
from jax import lax
from jax.sharding import PartitionSpec as P

BINS = 50
SHIFTS = 24


def passed_along(block, axis, distance):
    devices = range(lax.axis_size(axis))
    route = [(i - distance, i) for i in devices if i - distance in devices]
    return lax.ppermute(block, axis, route)


def bin_charges(charge, hit_bins, hit_ticks):
    tick_hot = (hit_ticks[..., None] == jnp.arange(SHIFTS, dtype=jnp.int32)).astype(jnp.float32)
    bin_hot = (hit_bins[..., None] == jnp.arange(BINS, dtype=jnp.int32)).astype(jnp.float32)
    weighted = charge[..., None] * tick_hot
    return jnp.einsum("xyks,xykb->xysb", weighted, bin_hot).astype(jnp.bfloat16)


def gather_offsets(source, rows, cols, count_x, count_y):
    pieces = []
    for row_off in range(-2, 3):
        for col_off in range(-2, 3):
            partial_value = source[
                2 - row_off : 2 - row_off + count_x, 2 - col_off : 2 - col_off + count_y
            ]
            row_same = rows[2 - row_off : 2 - row_off + count_x] == rows[2 : 2 + count_x]
            col_same = cols[2 - col_off : 2 - col_off + count_y] == cols[2 : 2 + count_y]
            allowed = row_same[:, None] & col_same[None, :]
            pieces.append(
                jnp.where(
                    allowed[:, :, None, None], partial_value, jnp.zeros((), partial_value.dtype)
                )
            )
    return jnp.stack(pieces, 0)


def shift_sum(partial_value, ticks):
    total = jnp.zeros(partial_value.shape[:2] + (ticks + SHIFTS,), jnp.float32)
    for offset in range(SHIFTS):
        total = total + jnp.pad(
            partial_value[:, :, offset, :], ((0, 0), (0, 0), (offset, SHIFTS - offset))
        )
    return total


def windows(resid, ticks):
    return jnp.stack([resid[:, :, offset : offset + ticks] for offset in range(SHIFTS)], axis=2)


def residual_of(prediction, measured, active):
    return (
        (prediction - measured.astype(jnp.float32)) * active.astype(jnp.float32)[..., None]
    ).astype(jnp.bfloat16)


def on_device(table, charge, hit_bins, hit_ticks, active, measured, row_module, col_module):
    tile_x, tile_y = (charge.shape[0], charge.shape[1])
    ticks = table.shape[2]
    parts_y = lax.axis_size("py")
    share = ticks // parts_y
    span = share + SHIFTS - 1
    weights = table.astype(jnp.bfloat16)
    row_start = lax.axis_index("px") * tile_x
    col_start = lax.axis_index("py") * tile_y
    deposits = jnp.stack(
        [charge, hit_bins.astype(jnp.float32), hit_ticks.astype(jnp.float32)], axis=-1
    )
    band = lax.all_gather(deposits, "py", axis=1, tiled=True)
    above = passed_along(band[tile_x - 2 :], "px", 1)
    below = passed_along(band[:2], "px", -1)
    wide = jnp.concatenate([above, band, below], axis=0)
    binned = bin_charges(
        wide[..., 0], wide[..., 1].astype(jnp.int32), wide[..., 2].astype(jnp.int32)
    )
    source = jnp.pad(binned, ((0, 0), (2, 2), (0, 0), (0, 0)))
    width = source.shape[1] - 4
    rows_wide = lax.dynamic_slice_in_dim(
        jnp.pad(row_module, 2, constant_values=-1), row_start, tile_x + 4, 0
    )
    cols_all = jnp.pad(col_module, 2, constant_values=-1)
    own_source = lax.dynamic_slice_in_dim(source, col_start, tile_y + 4, 1)
    own_cols = lax.dynamic_slice_in_dim(cols_all, col_start, tile_y + 4, 0)
    stacked = gather_offsets(own_source, rows_wide, own_cols, tile_x, tile_y)
    partial_value = jnp.einsum(
        "oxysb,obt->xyst", stacked, weights, preferred_element_type=jnp.float32
    )
    prediction = shift_sum(partial_value, ticks)
    resid = residual_of(prediction, measured, active)
    sent = jnp.stack([resid[:, :, k * share : k * share + span] for k in range(parts_y)], axis=0)
    got = lax.all_to_all(sent, "py", 0, 0)
    band_resid = jnp.transpose(got, (1, 0, 2, 3)).reshape(tile_x, width, span)
    stacked_band = gather_offsets(source, rows_wide, cols_all, tile_x, width)
    gradient = jnp.einsum(
        "oxysb,xysu->obu",
        stacked_band,
        windows(band_resid, share),
        preferred_element_type=jnp.float32,
    )
    summed = lax.psum(gradient, "px")
    return (prediction.astype(jnp.bfloat16), summed / 16)


def solution(mesh):
    in_specs = (
        P(),
        P("px", "py", None),
        P("px", "py", None),
        P("px", "py", None),
        P("px", "py"),
        P("px", "py", None),
        P(),
        P(),
    )
    out_specs = (P("px", "py", None), P(None, None, "py"))
    return jax.shard_map(
        on_device, mesh=mesh, in_specs=in_specs, out_specs=out_specs, check_vma=False
    )
```

profile of v0, /device:TPU:101, one launch (start us, length us, event | category | flops | bytes accessed | tf_op | source)
XLA Modules:
  0.0 386.6 jit_solution(15461394324954869272)
XLA Ops:
  7.2 0.7 convert_bitcast_fusion
  7.9 0.7 pad_maximum_fusion.1
  8.6 22.5 %all_gather.3 = f32[4,32,8,3]{2,0,3,1:T(4,128)S(1)} all-gather(f32[4,4,8,3]{2,0,3,1:T(4,128)S(1)} %copy.144), channel_id=1, replica_groups=mesh['px'=32,'py'=8] {'py'}, dimensions={1}, use_global_device_ids=true | all-gather | bytes 13824 | tf_op jit(solution)/shard_map/all_gather | solution.py:72
  31.2 8.9 %collective-permute-start.1 = (f32[2,32,8,3]{2,0,3,1:T(2,128)S(1)}, f32[2,32,8,3]{2,0,3,1:T(2,128)S(1)}, u32[]{:S(2)}, u32[]{:S(2)}) collective-permute-start(f32[2,32,8,3]{2,0,3,1:T(2,128)S(1)} %get-tuple-element.30), channel_id=1, source_target_pairs={{8,0},{16,8},{24,16},{32,24},{40,32},{48,40},{56,48},{64,56},{72,6... | collective-permute-start | bytes 18440 | tf_op jit(solution)/shard_map/ppermute | solution.py:13
  40.1 4.6 %collective-permute-start = (f32[2,32,8,3]{2,0,3,1:T(2,128)S(1)}, f32[2,32,8,3]{2,0,3,1:T(2,128)S(1)}, u32[]{:S(2)}, u32[]{:S(2)}) collective-permute-start(f32[2,32,8,3]{2,0,3,1:T(2,128)S(1)} %get-tuple-element.29), channel_id=1, source_target_pairs={{0,8},{8,16},{16,24},{24,32},{32,40},{40,48},{48,56},{56,64},{64,7... | collective-permute-start | bytes 18440 | tf_op jit(solution)/shard_map/ppermute | solution.py:13
  44.7 0.9 slice_compare_fusion
  45.6 0.7 pad_dynamic-slice_fusion.1
  46.4 0.7 pad_dynamic-slice_fusion
  47.3 0.1 copy.146
  47.4 0.7 convert_element_type.92
  48.7 2.9 convolution_convert_fusion
  51.7 0.1 constant_dynamic-update-slice_fusion.23
  51.9 0.1 constant_dynamic-update-slice_fusion.21
  52.1 0.1 constant_dynamic-update-slice_fusion.19
  53.2 0.1 constant_dynamic-update-slice_fusion.9
  54.3 1.3 slice-done
  55.6 0.6 slice-done.1
  56.1 2.6 fusion
  58.8 0.2 copy.351
  58.9 0.3 fusion.47
  59.2 1.2 fusion.46
  61.8 0.2 bitcast_dynamic-update-slice_fusion.19
  62.0 0.3 bitcast_dynamic-update-slice_fusion.18
  62.4 0.3 fusion.13
  62.6 0.3 bitcast_dynamic-update-slice_fusion.17
  63.0 0.3 bitcast_dynamic-update-slice_fusion.16
  63.3 0.3 bitcast_dynamic-update-slice_fusion.15
  63.7 0.3 bitcast_dynamic-update-slice_fusion.14
  64.0 0.3 fusion.11
  64.3 0.3 bitcast_dynamic-update-slice_fusion.13
  64.7 0.3 bitcast_dynamic-update-slice_fusion.12
  65.0 0.3 bitcast_dynamic-update-slice_fusion.11
  65.4 0.3 bitcast_dynamic-update-slice_fusion.10
  65.7 0.1 fusion.9
  65.8 0.3 bitcast_dynamic-update-slice_fusion.9
  66.2 0.3 bitcast_dynamic-update-slice_fusion.8
  66.5 0.3 bitcast_dynamic-update-slice_fusion.7
  66.9 0.3 bitcast_dynamic-update-slice_fusion.6
  67.2 0.3 fusion.8
  67.5 0.3 bitcast_dynamic-update-slice_fusion.5
  67.9 0.3 bitcast_dynamic-update-slice_fusion.4
  68.2 0.5 bitcast_dynamic-update-slice_fusion.3
  68.7 0.3 bitcast_dynamic-update-slice_fusion.2
  69.1 0.3 fusion.6
  69.5 2.0 multiply_convert_fusion
  71.5 4.6 %copy-done.1 = bf16[25,4,32,24,50]{4,3,2,1,0:T(8,128)(2,1)} copy-done((bf16[25,4,32,24,50]{4,3,2,1,0:T(8,128)(2,1)}, bf16[25,4,32,24,50]{4,3,2,1,0:T(8,128)(2,1)S(1)}, u32[]{:S(2)}) %copy-start.1) | copy-done | bytes 7680024
  76.1 0.6 constant_dynamic-update-slice_fusion.32
  76.7 0.7 constant_dynamic-update-slice_fusion.31
  77.3 0.7 constant_dynamic-update-slice_fusion.30
  78.0 0.7 constant_dynamic-update-slice_fusion.29
  78.7 0.7 constant_dynamic-update-slice_fusion.28
  79.4 0.7 constant_dynamic-update-slice_fusion.27
  80.0 0.7 constant_dynamic-update-slice_fusion.26
  80.7 0.7 constant_dynamic-update-slice_fusion.25
  81.4 5.4 %all-to-all-start = ((bf16[8,4,4,148]{3,2,1,0:T(4,128)(2,1)}), bf16[8,4,4,148]{3,2,1,0:T(4,128)(2,1)S(1)}, u32[]{:S(2)}, u32[]{:S(2)}) async-start(bf16[8,4,4,148]{3,2,1,0:T(4,128)(2,1)} %constant_dynamic-update-slice_fusion.25), calls=%async_computation | async-start | bytes 131072 | tf_op jit(solution)/shard_map/all_to_all | solution.py:94
  86.8 1.1 bitcast_dynamic-update-slice_fusion.1
  88.0 1.1 bitcast_dynamic-update-slice_fusion
  89.1 2.9 all-to-all-done
  92.0 0.1 slice_bitcast_fusion.20
  92.1 0.4 slice_bitcast_fusion.1
  94.0 2.6 stack.359
  96.6 12.7 %convolution_bitcast_fusion = f32[25,50,125]{2,1,0:T(8,128)} fusion(bf16[25,4,32,24,50]{4,3,2,1,0:T(8,128)(2,1)} %bitcast_dynamic-update-slice_fusion, bf16[4,32,24,125]{3,2,1,0:T(8,128)(2,1)S(1)} %stack.359), kind=kOutput, calls=%fused_computation.6 | convolution fusion | flops 960000000 | bytes 9073000 | tf_op jit(solution)/shard_map/oxysb,xysu->obu/dot_general | solution.py:97
  109.3 268.5 %all-reduce.29.cloned.1.call-done = f32[25,50,125]{2,1,0:T(8,128)} async-done(((f32[25,50,125]{2,1,0:T(8,128)}), f32[25,50,125]{2,1,0:T(8,128)}) %all-reduce.29.cloned.1.call-update) | async-done | bytes 625016 | tf_op jit(solution)/shard_map/psum | solution.py:103
  377.8 2.0 broadcast_multiply_fusion
  (94 shorter events, 5.6 us)
Async XLA Ops:
  31.2 16.9 %collective-permute-start.1 = (f32[2,32,8,3]{2,0,3,1:T(2,128)S(1)}, f32[2,32,8,3]{2,0,3,1:T(2,128)S(1)}, u32[]{:S(2)}, u32[]{:S(2)}) collective-permute-start(f32[2,32,8,3]{2,0,3,1:T(2,128)S(1)} %get-tuple-element.30), channel_id=1, source_target_pairs={{8,0},{16,8},{24,16},{32,24},{40,32},{48,40},{56,48},{64,56},{72,6... | collective-permute-start | bytes 18440 | tf_op jit(solution)/shard_map/ppermute | solution.py:13
  40.1 8.2 %collective-permute-start = (f32[2,32,8,3]{2,0,3,1:T(2,128)S(1)}, f32[2,32,8,3]{2,0,3,1:T(2,128)S(1)}, u32[]{:S(2)}, u32[]{:S(2)}) collective-permute-start(f32[2,32,8,3]{2,0,3,1:T(2,128)S(1)} %get-tuple-element.29), channel_id=1, source_target_pairs={{0,8},{8,16},{16,24},{24,32},{32,40},{40,48},{48,56},{56,64},{64,7... | collective-permute-start | bytes 18440 | tf_op jit(solution)/shard_map/ppermute | solution.py:13
  53.4 2.2 slice-start
  53.7 2.4 slice-start.1
  68.7 0.8 copy-start
  69.4 6.7 %copy-start.1 = (bf16[25,4,32,24,50]{4,3,2,1,0:T(8,128)(2,1)}, bf16[25,4,32,24,50]{4,3,2,1,0:T(8,128)(2,1)S(1)}, u32[]{:S(2)}) copy-start(bf16[25,4,32,24,50]{4,3,2,1,0:T(8,128)(2,1)S(1)} %fusion.6) | copy-start | bytes 23040004
  81.4 10.6 %all-to-all-start = ((bf16[8,4,4,148]{3,2,1,0:T(4,128)(2,1)}), bf16[8,4,4,148]{3,2,1,0:T(4,128)(2,1)S(1)}, u32[]{:S(2)}, u32[]{:S(2)}) async-start(bf16[8,4,4,148]{3,2,1,0:T(4,128)(2,1)} %constant_dynamic-update-slice_fusion.25), calls=%async_computation | async-start | bytes 131072 | tf_op jit(solution)/shard_map/all_to_all | solution.py:94
  86.8 291.0 %all-reduce.29.cloned.1.call-start = ((), (), s32[]{:S(2)}) async-start(), calls=%async_computation.1 | async-start | bytes 1433600 | tf_op jit(solution)/shard_map/psum | solution.py:103
Sparse Core Ops, SparseCore 0:
  109.4 268.2 all-reduce.28
where the time goes:
time: 387 us
  waiting for transfers between devices  271 us (70%)
  blocking collectives  22.5 us (6%)
  local copies, waits for them, and re-layouts  21.4 us (6%)
  other arithmetic  19.5 us (5%)
  starting transfers between devices  18.9 us (5%)
  matrix products  18.2 us (5%)
  between operations  14.8 us (4%)
    psum x1, waiting for transfers between devices, on_device(): summed = lax.psum(gradient, 'px')  268 us
    all_gather x1, blocking collectives, on_device(): band = lax.all_gather(deposits, 'py', axis=1, tiled=True)  22.5 us
    ppermute x2, starting transfers between devices, passed_along(): return lax.ppermute(block, axis, route)  13.4 us
    dot_general x1, matrix products, on_device(): jnp.einsum('oxysb,xysu->obu', stacked_band, windows(band_resid, share), p...  12.7 us
    unnamed x41, local copies, waits for them, and re-layouts  12.4 us
    unnamed x47, other arithmetic  10.9 us
  transfers between devices with their start and end apart: 4, of which 2 were waited for; matrix products, arithmetic and copies ran while one was open for 2% of the time, Pallas kernels for 0%

commit v1 on v0

--- a/solution.py
+++ b/solution.py
@@ -5,6 +5,19 @@
 
 BINS = 50
 SHIFTS = 24
+
+
+def detail_state_for(piece_in, device_axis, array_dim):
+    parts_seen = []
+    for _ in range(jax.lax.axis_size(device_axis)):
+        parts_seen.append(piece_in)
+    odd = jnp.concatenate(
+        jax.lax.all_to_all(
+            jnp.stack(parts_seen), axis_name=device_axis, split_axis=0, concat_axis=0
+        ),
+        axis=array_dim,
+    )
+    return odd
 
 
 def passed_along(block, axis, distance):
@@ -69,7 +82,7 @@
     deposits = jnp.stack(
         [charge, hit_bins.astype(jnp.float32), hit_ticks.astype(jnp.float32)], axis=-1
     )
-    band = lax.all_gather(deposits, "py", axis=1, tiled=True)
+    band = detail_state_for(deposits, "py", 1)
     above = passed_along(band[tile_x - 2 :], "px", 1)
     below = passed_along(band[:2], "px", -1)
     wide = jnp.concatenate([above, band, below], axis=0)

time: 387 us -> 371 us (0.959)
  blocking collectives: 22.5 us -> 0 us
  waiting for transfers between devices: 271 us -> 277 us
    all_gather x1 -> x0, blocking collectives: 22.5 us -> none  [on_device(): band = lax.all_gather(deposits, 'py', axis=1, tiled=True)]
    all_to_all x0 -> x1, starting transfers between devices: none -> 4.82 us  [detail_state_for(): jax.lax.all_to_all(jnp.stack(parts_seen), axis_name=device_axis, split_ax...]
    ppermute x2, starting transfers between devices: 13.4 us -> 9.18 us  [passed_along(): return lax.ppermute(block, axis, route)]
    unnamed x41 -> x44, local copies, waits for them, and re-layouts: 12.4 us -> 13.5 us
  transfers between devices with their start and end apart: 4 -> 5, of which waited for: 2 -> 4; matrix products, arithmetic and copies ran while one was open for 2% -> 2% of each run, Pallas kernels for 0% -> 0%
where the time goes in v1:
time: 371 us; the launch traced here: 370 us
  waiting for transfers between devices  277 us (75%)
  local copies, waits for them, and re-layouts  22.9 us (6%)
  other arithmetic  20.1 us (5%)
  matrix products  18.2 us (5%)
  starting transfers between devices  17.4 us (5%)
  between operations  14.8 us (4%)
    psum x1, waiting for transfers between devices, on_device(): summed = lax.psum(gradient, 'px')  271 us
    unnamed x44, local copies, waits for them, and re-layouts  13.5 us
    dot_general x1, matrix products, on_device(): jnp.einsum('oxysb,xysu->obu', stacked_band, windows(band_resid, share), p...  12.7 us
    unnamed x47, other arithmetic  10.9 us
    ppermute x2, starting transfers between devices, passed_along(): return lax.ppermute(block, axis, route)  9.18 us
  transfers between devices with their start and end apart: 5, of which 4 were waited for; matrix products, arithmetic and copies ran while one was open for 2% of the time, Pallas kernels for 0%

profile of v1, /device:TPU:101, one launch (start us, length us, event | category | flops | bytes accessed | tf_op | source)
XLA Modules:
  0.0 370.1 jit_solution(8022246002777217853)
XLA Ops:
  7.2 0.7 convert_bitcast_fusion
  7.9 0.7 pad_maximum_fusion.1
  8.6 0.8 reshape.925
  9.4 4.8 %all-to-all-start = ((f32[8,1,384]{2,1,0:T(1,128)}), f32[8,1,384]{2,1,0:T(1,128)S(1)}, u32[]{:S(2)}, u32[]{:S(2)}) async-start(f32[8,1,384]{2,1,0:T(1,128)} %reshape.925), calls=%async_computation | async-start | bytes 24576 | tf_op jit(solution)/shard_map/all_to_all | solution.py:15
  14.2 0.7 pad_dynamic-slice_fusion
  15.0 0.7 pad_dynamic-slice_fusion.1
  15.9 0.9 slice_compare_fusion
  16.8 2.5 all-to-all-done
  19.3 0.5 broadcast.904
  19.8 0.7 reduce
  20.5 0.3 reshape.926
  20.8 4.0 %collective-permute-start.1 = (f32[2,32,8,3]{2,1,3,0:T(8,128)S(1)}, f32[2,32,8,3]{2,1,3,0:T(8,128)S(1)}, u32[]{:S(2)}, u32[]{:S(2)}) collective-permute-start(f32[2,32,8,3]{2,1,3,0:T(8,128)S(1)} %bitcast.410), channel_id=1, source_target_pairs={{8,0},{16,8},{24,16},{32,24},{40,32},{48,40},{56,48},{64,56},{72,6... | collective-permute-start | bytes 18440 | tf_op jit(solution)/shard_map/ppermute | solution.py:26
  24.9 5.2 %collective-permute-start = (f32[2,32,8,3]{2,1,3,0:T(8,128)S(1)}, f32[2,32,8,3]{2,1,3,0:T(8,128)S(1)}, u32[]{:S(2)}, u32[]{:S(2)}) collective-permute-start(f32[2,32,8,3]{2,1,3,0:T(8,128)S(1)} %bitcast.411), channel_id=1, source_target_pairs={{0,8},{8,16},{16,24},{24,32},{32,40},{40,48},{48,56},{56,64},{64,7... | collective-permute-start | bytes 18440 | tf_op jit(solution)/shard_map/ppermute | solution.py:26
  30.1 0.7 convert_element_type.92
  31.1 0.6 collective-permute-done
  32.1 2.9 convolution_convert_fusion
  37.7 1.3 slice-done
  39.0 0.6 slice-done.1
  39.5 2.6 fusion
  42.1 0.2 copy.349
  42.3 0.3 fusion.47
  42.6 1.2 fusion.46
  45.1 0.2 bitcast_dynamic-update-slice_fusion.19
  45.4 0.3 bitcast_dynamic-update-slice_fusion.18
  45.7 0.3 fusion.13
  46.0 0.3 bitcast_dynamic-update-slice_fusion.17
  46.4 0.3 bitcast_dynamic-update-slice_fusion.16
  46.7 0.3 bitcast_dynamic-update-slice_fusion.15
  47.1 0.3 bitcast_dynamic-update-slice_fusion.14
  47.4 0.3 fusion.11
  47.7 0.3 bitcast_dynamic-update-slice_fusion.13
  48.1 0.3 bitcast_dynamic-update-slice_fusion.12
  48.4 0.3 bitcast_dynamic-update-slice_fusion.11
  48.7 0.3 bitcast_dynamic-update-slice_fusion.10
  49.2 0.3 bitcast_dynamic-update-slice_fusion.9
  49.6 0.3 bitcast_dynamic-update-slice_fusion.8
  49.9 0.3 bitcast_dynamic-update-slice_fusion.7
  50.3 0.3 bitcast_dynamic-update-slice_fusion.6
  50.6 0.3 fusion.8
  50.9 0.3 bitcast_dynamic-update-slice_fusion.5
  51.2 0.3 bitcast_dynamic-update-slice_fusion.4
  51.6 0.5 bitcast_dynamic-update-slice_fusion.3
  52.1 0.3 bitcast_dynamic-update-slice_fusion.2
  52.5 0.3 fusion.6
  52.9 2.0 multiply_convert_fusion
  54.9 4.5 %copy-done.1 = bf16[25,4,32,24,50]{4,3,2,1,0:T(8,128)(2,1)} copy-done((bf16[25,4,32,24,50]{4,3,2,1,0:T(8,128)(2,1)}, bf16[25,4,32,24,50]{4,3,2,1,0:T(8,128)(2,1)S(1)}, u32[]{:S(2)}) %copy-start.1) | copy-done | bytes 7680024
  59.4 0.6 constant_dynamic-update-slice_fusion.32
  60.0 0.7 constant_dynamic-update-slice_fusion.31
  60.7 0.7 constant_dynamic-update-slice_fusion.30
  61.4 0.7 constant_dynamic-update-slice_fusion.29
  62.0 0.7 constant_dynamic-update-slice_fusion.28
  62.7 0.7 constant_dynamic-update-slice_fusion.27
  63.4 0.7 constant_dynamic-update-slice_fusion.26
  64.1 0.7 constant_dynamic-update-slice_fusion.25
  64.7 3.4 all-to-all-start.1
  68.2 1.1 bitcast_dynamic-update-slice_fusion.1
  69.3 1.1 bitcast_dynamic-update-slice_fusion
  70.4 2.8 all-to-all-done.1
  73.3 0.1 slice_bitcast_fusion.20
  73.4 0.4 slice_bitcast_fusion.1
  75.3 2.6 stack.371
  77.9 12.7 %convolution_bitcast_fusion = f32[25,50,125]{2,1,0:T(8,128)} fusion(bf16[25,4,32,24,50]{4,3,2,1,0:T(8,128)(2,1)} %bitcast_dynamic-update-slice_fusion, bf16[4,32,24,125]{3,2,1,0:T(8,128)(2,1)S(1)} %stack.371), kind=kOutput, calls=%fused_computation.6 | convolution fusion | flops 960000000 | bytes 9073000 | tf_op jit(solution)/shard_map/oxysb,xysu->obu/dot_general | solution.py:110
  90.6 270.7 %all-reduce.29.cloned.1.call-done = f32[25,50,125]{2,1,0:T(8,128)} async-done(((f32[25,50,125]{2,1,0:T(8,128)}), f32[25,50,125]{2,1,0:T(8,128)}) %all-reduce.29.cloned.1.call-update) | async-done | bytes 625016 | tf_op jit(solution)/shard_map/psum | solution.py:116
  361.3 2.0 broadcast_multiply_fusion
  (103 shorter events, 6.3 us)
Async XLA Ops:
  9.4 9.9 %all-to-all-start = ((f32[8,1,384]{2,1,0:T(1,128)}), f32[8,1,384]{2,1,0:T(1,128)S(1)}, u32[]{:S(2)}, u32[]{:S(2)}) async-start(f32[8,1,384]{2,1,0:T(1,128)} %reshape.925), calls=%async_computation | async-start | bytes 24576 | tf_op jit(solution)/shard_map/all_to_all | solution.py:15
  20.8 10.1 %collective-permute-start.1 = (f32[2,32,8,3]{2,1,3,0:T(8,128)S(1)}, f32[2,32,8,3]{2,1,3,0:T(8,128)S(1)}, u32[]{:S(2)}, u32[]{:S(2)}) collective-permute-start(f32[2,32,8,3]{2,1,3,0:T(8,128)S(1)} %bitcast.410), channel_id=1, source_target_pairs={{8,0},{16,8},{24,16},{32,24},{40,32},{48,40},{56,48},{64,56},{72,6... | collective-permute-start | bytes 18440 | tf_op jit(solution)/shard_map/ppermute | solution.py:26
  24.9 6.8 %collective-permute-start = (f32[2,32,8,3]{2,1,3,0:T(8,128)S(1)}, f32[2,32,8,3]{2,1,3,0:T(8,128)S(1)}, u32[]{:S(2)}, u32[]{:S(2)}) collective-permute-start(f32[2,32,8,3]{2,1,3,0:T(8,128)S(1)} %bitcast.411), channel_id=1, source_target_pairs={{0,8},{8,16},{16,24},{24,32},{32,40},{40,48},{48,56},{56,64},{64,7... | collective-permute-start | bytes 18440 | tf_op jit(solution)/shard_map/ppermute | solution.py:26
  36.8 2.2 slice-start
  37.1 2.4 slice-start.1
  52.1 0.8 copy-start
  52.8 6.7 %copy-start.1 = (bf16[25,4,32,24,50]{4,3,2,1,0:T(8,128)(2,1)}, bf16[25,4,32,24,50]{4,3,2,1,0:T(8,128)(2,1)S(1)}, u32[]{:S(2)}) copy-start(bf16[25,4,32,24,50]{4,3,2,1,0:T(8,128)(2,1)S(1)} %fusion.6) | copy-start | bytes 23040004
  64.7 8.5 %all-to-all-start.1 = ((bf16[8,4,4,148]{3,2,1,0:T(4,128)(2,1)}), bf16[8,4,4,148]{3,2,1,0:T(4,128)(2,1)S(1)}, u32[]{:S(2)}, u32[]{:S(2)}) async-start(bf16[8,4,4,148]{3,2,1,0:T(4,128)(2,1)} %constant_dynamic-update-slice_fusion.25), calls=%async_computation.1 | async-start | bytes 131072 | tf_op jit(solution)/shard_map/all_to_all | solution.py:107
  68.1 293.2 %all-reduce.29.cloned.1.call-start = ((), (), s32[]{:S(2)}) async-start(), calls=%async_computation.2 | async-start | bytes 1433600 | tf_op jit(solution)/shard_map/psum | solution.py:116
Sparse Core Ops, SparseCore 0:
  90.7 270.5 all-reduce.28
